TPU v7x, 128 devices: a whole 4x4x4 slice. The times are simulated.
128 devices in a mesh: seq: 32 (over x, z, core), mp: 4 (over y).
Axes of the slice: x: 4, y: 4, z: 4, core: 2. Of those that a mesh axis runs over, the one named last changes fastest.
Arguments:
- hidden: bfloat16 [16384, 4096], P('seq', 'mp'), may hold values from -6 to 6
- w_zx: bfloat16 [4096, 2, 4096], P(None, None, 'mp'), may hold values from -0.09375 to 0.09375
- w_bc: bfloat16 [4096, 2, 512], P(None, None, 'mp'), may hold values from -0.09375 to 0.09375
- w_dt: bfloat16 [4096, 64], P(None, 'mp'), may hold values from -0.09375 to 0.09375
- conv_x: float32 [4, 4096], P(None, 'mp'), may hold values from -3 to 3
- conv_x_bias: float32 [4096], P('mp'), may hold values from -3 to 3
- conv_bc: float32 [4, 2, 512], P(None, None, 'mp'), may hold values from -3 to 3
- conv_bc_bias: float32 [2, 512], P(None, 'mp'), may hold values from -3 to 3
- a_log: float32 [64], P('mp'), may hold values from -9.5 to -0.5
- dt_bias: float32 [64], P('mp'), may hold values from -4 to -1
- d_skip: float32 [64], P('mp'), may hold values from 0.5 to 4
- norm_gain: float32 [4096], P('mp'), may hold values from 0.4 to 1.6
- state_bank: float32 [2, 64, 64, 128], P(None, 'mp'), may hold values from -2 to 2
- conv_bank_x: bfloat16 [2, 3, 4096], P(None, None, 'mp'), may hold values from -5 to 5
- conv_bank_bc: bfloat16 [2, 3, 2, 512], P(None, None, None, 'mp'), may hold values from -5 to 5
- prompt_blocks: int32 [9], replicated, may hold values from 1 to 48, 64 in all
- prompt_order: int32 [9], replicated, may hold values from 0 to 8, each once
- resume_slot: int32 [9], replicated, may hold values from 0 to 2
Outputs:
- mixed: bfloat16 [16384, 4096], P('seq', 'mp')
Inputs may be any that keep to these rules, and one draw needn't show every extreme that they name: `prompt_blocks`: blocks of each prompt; they sum to 64 and the longest is exactly 48. `prompt_order`: A permutation of the prompts. `resume_slot`: 2 means a fresh start from zero state and zero convolution rows.
All inputs are finite; a program needn't handle non-finite values.
Results may differ from a plain program's by a relative error of at most 0.0068.
Values may be sent and summed in bfloat16 or wider, within the bound.
No kernel may reach another device: no remote copies, remote signals or barrier semaphores. Data moves between devices by JAX's collectives and lax.ppermute only.
A program may use at most 192 MiB of HBM per device.

v0:
```python
import jax
import jax.numpy as jnp
from jax import lax
from jax.sharding import PartitionSpec as P

WIDTH = 4096
HEAD_DIM = 64
STATE = 128
BLOCK = 256
KERNEL = 4
BANK = 2


def from_behind(value, axis, steps):
    count = lax.axis_size(axis)
    pairs = [(source, (source + steps) % count) for source in range(count)]
    return lax.ppermute(value, axis, pairs)


def combine(earlier, later):
    return (earlier[0] * later[0], later[0][:, None, None] * earlier[1] + later[1])


def per_device(
    hidden,
    w_zx,
    w_bc,
    w_dt,
    conv_x,
    conv_x_bias,
    conv_bc,
    conv_bc_bias,
    a_log,
    dt_bias,
    d_skip,
    norm_gain,
    state_bank,
    conv_bank_x,
    conv_bank_bc,
    prompt_blocks,
    prompt_order,
    resume_slot,
):
    devices = lax.axis_size("seq")
    place = lax.axis_index("seq")
    rows_dev = hidden.shape[0]
    blocks = rows_dev // BLOCK
    inner_dev = w_zx.shape[2]
    gstate_dev = w_bc.shape[2]
    heads_dev = w_dt.shape[1]
    groups_dev = gstate_dev // STATE
    per_group = heads_dev // groups_dev
    channels = inner_dev + 2 * gstate_dev
    prompts = prompt_blocks.shape[0]
    flat_zx = w_zx.reshape(WIDTH, 2 * inner_dev)
    flat_bc = w_bc.reshape(WIDTH, 2 * gstate_dev)
    piece = lax.all_gather(hidden, "mp", axis=1, tiled=True)
    zx_sum = jnp.dot(piece, flat_zx, preferred_element_type=jnp.float32)
    bc_sum = jnp.dot(piece, flat_bc, preferred_element_type=jnp.float32)
    dt_raw = jnp.dot(piece, w_dt, preferred_element_type=jnp.float32)
    zx = zx_sum.astype(jnp.bfloat16)
    bc = bc_sum.astype(jnp.bfloat16)
    gate = zx[:, :inner_dev]
    mixin = jnp.concatenate([zx[:, inner_dev:], bc], axis=1).reshape(blocks, BLOCK, channels)
    own_tails = mixin[:, BLOCK - (KERNEL - 1) :, :]
    arrived = from_behind(own_tails, "seq", 1)
    wrapped = jnp.concatenate([jnp.zeros_like(arrived[:1]), arrived[:-1]], axis=0)
    before = jnp.where(place > 0, arrived, wrapped)
    prompt_ids = jnp.arange(prompts, dtype=jnp.int32)
    order_hot = (prompt_order[:, None] == prompt_ids[None, :]).astype(jnp.int32)
    lengths = jnp.sum(order_hot * prompt_blocks[None, :], axis=1)
    slots = jnp.sum(order_hot * resume_slot[None, :], axis=1)
    ends = jnp.cumsum(lengths)
    starts = ends - lengths
    stream_ids = jnp.arange(blocks, dtype=jnp.int32) * devices + place
    inside = (
        (stream_ids[:, None] >= starts[None, :]) & (stream_ids[:, None] < ends[None, :])
    ).astype(jnp.int32)
    block_slot = jnp.sum(inside * slots[None, :], axis=1)
    first = jnp.any(stream_ids[:, None] == starts[None, :], axis=1)
    pick = (block_slot[:, None] == jnp.arange(BANK, dtype=jnp.int32)[None, :]).astype(jnp.float32)
    bank_state = jnp.einsum("cr,rhpn->chpn", pick, state_bank, precision=lax.Precision.HIGHEST)
    bank_rows = jnp.concatenate(
        [conv_bank_x, conv_bank_bc.reshape(BANK, KERNEL - 1, 2 * gstate_dev)], axis=2
    )
    bank_tail = jnp.einsum("cr,rkz->ckz", pick, bank_rows.astype(jnp.float32)).astype(jnp.bfloat16)
    tail = jnp.where(first[:, None, None], bank_tail, before)
    kernel = jnp.concatenate([conv_x, conv_bc.reshape(KERNEL, 2 * gstate_dev)], axis=1)
    bias = jnp.concatenate([conv_x_bias, conv_bc_bias.reshape(2 * gstate_dev)], axis=0)
    padded = jnp.concatenate([tail, mixin], axis=1).astype(jnp.float32)
    acc = bias[None, None, :] + padded[:, 0:BLOCK] * kernel[0]
    for k in range(1, KERNEL):
        acc = acc + padded[:, k : k + BLOCK] * kernel[k]
    conv = jax.nn.silu(acc).astype(jnp.bfloat16)
    xs = conv[..., :inner_dev].reshape(blocks, BLOCK, groups_dev, per_group, HEAD_DIM)
    bs = conv[..., inner_dev : inner_dev + gstate_dev].reshape(blocks, BLOCK, groups_dev, STATE)
    cq = conv[..., inner_dev + gstate_dev :].reshape(blocks, BLOCK, groups_dev, STATE)
    dt = jax.nn.softplus(dt_raw.reshape(blocks, BLOCK, heads_dev) + dt_bias[None, None, :])
    cum = jnp.cumsum(dt * (-jnp.exp(a_log))[None, None, :], axis=1)
    scores = jnp.einsum("cqgn,ckgn->cgqk", cq, bs, preferred_element_type=jnp.float32)
    cum_h = cum.transpose(0, 2, 1)
    lower = jnp.arange(BLOCK)[:, None] >= jnp.arange(BLOCK)[None, :]
    damp = jnp.exp(
        jnp.where(lower[None, None], cum_h[:, :, :, None] - cum_h[:, :, None, :], -jnp.inf)
    )
    damp = damp.reshape(blocks, groups_dev, per_group, BLOCK, BLOCK)
    dt_h = dt.transpose(0, 2, 1).reshape(blocks, groups_dev, per_group, 1, BLOCK)
    mix = (scores[:, :, None] * damp * dt_h).astype(jnp.bfloat16)
    y_intra = jnp.einsum("cgjqk,ckgjp->cqgjp", mix, xs, preferred_element_type=jnp.float32)
    last = cum[:, -1, :]
    grow = jnp.exp(last)
    factor = (dt * jnp.exp(last[:, None, :] - cum)).reshape(blocks, BLOCK, groups_dev, per_group, 1)
    weighted = (xs.astype(jnp.float32) * factor).astype(jnp.bfloat16)
    local_state = jnp.einsum(
        "cqgjp,cqgn->cgjpn", weighted, bs, preferred_element_type=jnp.float32
    ).reshape(blocks, heads_dev, HEAD_DIM, STATE)
    step_a = jnp.where(first[:, None], 0.0, grow)
    step_b = local_state + jnp.where(
        first[:, None, None, None], grow[:, :, None, None] * bank_state, 0.0
    )
    core = place % 2
    chip = place // 2
    chips = devices // 2
    half = heads_dev // 2
    rows = blocks * half

    def keep(part, at):
        piece = lax.dynamic_slice_in_dim(part, at * half, half, axis=1)
        return piece.reshape((rows,) + part.shape[2:])

    pair = [(source, source ^ 1) for source in range(devices)]
    mine = (keep(step_a, core), keep(step_b, core))
    got = lax.ppermute((keep(step_a, 1 - core), keep(step_b, 1 - core)), "seq", pair)
    early = jax.tree.map(lambda own, other: jnp.where(core == 0, own, other), mine, got)
    later = jax.tree.map(lambda own, other: jnp.where(core == 0, other, own), mine, got)
    quarter = half // 2
    split_heads = lambda part: [
        part.reshape((blocks, 2, quarter) + part.shape[1:])[:, g].reshape(
            (blocks * quarter,) + part.shape[1:]
        )
        for g in range(2)
    ]
    chip_a, chip_b = combine(early, later)
    lanes = [list(pair) for pair in zip(split_heads(chip_a), split_heads(chip_b))]
    priors = [[jnp.ones_like(lane[0]), jnp.zeros_like(lane[1])] for lane in lanes]

    def wrap(part, neutral, late):
        moved = jnp.concatenate(
            [jnp.full_like(part[:quarter], neutral), part[: part.shape[0] - quarter]], axis=0
        )
        return jnp.where(late, part, moved)

    span = 1
    while span < chips:
        late = chip >= span
        for g in range(2):
            got_a, got_b = from_behind(tuple(lanes[g]), "seq", 2 * span)
            lead = (wrap(got_a, 1.0, late), wrap(got_b, 0.0, late))
            lanes[g] = list(combine(lead, tuple(lanes[g])))
            priors[g] = list(combine(lead, tuple(priors[g])))
        span *= 2
    joined = []
    for g in range(2):
        run_a, run_b = lanes[g]
        prior_a, prior_b = priors[g]
        lift = combine((run_a[:quarter], run_b[:quarter]), (prior_a[quarter:], prior_b[quarter:]))[
            1
        ]
        joined.append(jnp.concatenate([prior_b[:quarter], lift], axis=0))
    before_chip = jnp.concatenate(
        [part.reshape((blocks, quarter) + part.shape[1:]) for part in joined], axis=1
    ).reshape(chip_b.shape)
    after_early = early[0][:, None, None] * before_chip + early[1]
    own_part = jnp.where(core == 0, before_chip, after_early)
    other_part = lax.ppermute(jnp.where(core == 0, after_early, before_chip), "seq", pair)
    split_rows = lambda part: part.reshape((blocks, half) + part.shape[1:])
    own_part, other_part = (split_rows(own_part), split_rows(other_part))
    previous = jnp.where(
        core == 0,
        jnp.concatenate([own_part, other_part], axis=1),
        jnp.concatenate([other_part, own_part], axis=1),
    )
    state_in = jnp.where(first[:, None, None, None], bank_state, previous)
    read = jnp.einsum(
        "cqgn,cgjpn->cqgjp",
        cq.astype(jnp.float32),
        state_in.reshape(blocks, groups_dev, per_group, HEAD_DIM, STATE),
        precision=lax.Precision.HIGHEST,
    )
    growth = jnp.exp(cum).reshape(blocks, BLOCK, groups_dev, per_group, 1)
    skip = d_skip.reshape(1, 1, groups_dev, per_group, 1)
    y_total = y_intra + growth * read + skip * xs.astype(jnp.float32)
    gated = y_total.reshape(rows_dev, inner_dev) * jax.nn.silu(gate.astype(jnp.float32))
    grouped = gated.reshape(rows_dev, groups_dev, inner_dev // groups_dev)
    scale = lax.rsqrt(jnp.mean(grouped * grouped, axis=2, keepdims=True) + 1e-05)
    result = (grouped * scale).reshape(rows_dev, inner_dev) * norm_gain[None, :]
    return result.astype(jnp.bfloat16)


def solution(mesh):
    placed = (
        P("seq", "mp"),
        P(None, None, "mp"),
        P(None, None, "mp"),
        P(None, "mp"),
        P(None, "mp"),
        P("mp"),
        P(None, None, "mp"),
        P(None, "mp"),
        P("mp"),
        P("mp"),
        P("mp"),
        P("mp"),
        P(None, "mp", None, None),
        P(None, None, "mp"),
        P(None, None, None, "mp"),
        P(),
        P(),
        P(),
    )
    return jax.shard_map(
        per_device, mesh=mesh, in_specs=placed, out_specs=P("seq", "mp"), check_vma=False
    )
```

profile of v0, /device:TPU:1, one launch (start us, length us, event | category | flops | bytes accessed | tf_op | source)
XLA Modules:
  0.0 195.6 jit_solution(3872452470648923946)
XLA Ops:
  7.3 0.9 select_reduce_fusion.1
  8.4 17.2 %copy.111 = bf16[512,8,2,1024]{3,1,2,0:T(8,128)(2,1)} copy(bf16[512,8,2,1024]{3,2,1,0:T(2,128)(2,1)} %bitcast.142) | data formatting | bytes 33554432
  26.2 34.1 %all-gather.2.cloned.1.call-done = bf16[512,4096]{1,0:T(8,128)(2,1)} async-done(((bf16[512,1024]{1,0:T(8,128)(2,1)}), bf16[512,4096]{1,0:T(8,128)(2,1)}) %all-gather.2.cloned.1.call-update) | async-done | bytes 4194320 | tf_op jit(solution)/shard_map/all_gather | solution.py:57
  60.3 15.8 %convolution_convert_fusion = bf16[512,2048]{1,0:T(8,128)(2,1)S(1)} fusion(bf16[512,4096]{1,0:T(8,128)(2,1)} %all-gather.2.cloned.1.call-done, bf16[4096,2048]{1,0:T(8,128)(2,1)} %bitcast.143), kind=kOutput, calls=%fused_computation.8 | convolution fusion | flops 8590983168 | bytes 23068672 | tf_op jit(solution)/shard_map/dot_general | solution.py:58
  76.2 2.2 %copy-done.16 = bf16[4096,2,128]{2,1,0:T(2,128)(2,1)S(1)} copy-done((bf16[4096,2,128]{2,1,0:T(2,128)(2,1)S(1)}, bf16[4096,2,128]{2,1,0:T(2,128)(2,1)}, u32[]{:S(2)}) %copy-start.16) | copy-done | bytes 2097176
  78.4 1.3 fusion.20
  79.9 2.1 %collective-permute-start = (bf16[2,3,1280]{2,0,1:T(2,128)(2,1)S(1)}, bf16[2,3,1280]{2,0,1:T(2,128)(2,1)S(1)}, u32[]{:S(2)}, u32[]{:S(2)}) collective-permute-start(bf16[2,3,1280]{2,0,1:T(2,128)(2,1)S(1)} %copy.107), channel_id=1, source_target_pairs={{0,4},{4,8},{8,12},{12,16},{16,20},{20,24},{24,28},{28,32},{32,36}... | collective-permute-start | bytes 46088 | tf_op jit(solution)/shard_map/ppermute | solution.py:17
  82.0 1.2 fusion.73
  83.3 1.2 reduce-window.18
  85.4 1.1 collective-permute-done.1
  86.7 1.3 collective-permute-start.2
  88.0 1.0 collective-permute-start.11
  89.5 1.7 multiply_convert_fusion.2
  91.2 1.4 slice_convert_fusion
  92.6 2.3 %copy.84 = bf16[2,256,1024]{1,2,0:T(8,128)(2,1)} copy(bf16[2,256,1024]{2,1,0:T(8,128)(2,1)} %get-tuple-element.33) | data formatting | bytes 2097152 | tf_op jit(solution)/shard_map/slice | solution.py:95
  94.9 1.7 fusion.23
  96.6 4.6 %copy_add_fusion = (f32[2,16,64,128]{3,0,2,1:T(2,128)S(1)}, f32[2,16,64,128]{3,0,2,1:T(2,128)}) fusion(f32[2,16,64,128]{3,2,1,0:T(8,128)S(1)} %fusion.23, pred[2]{0:T(512)(128)(4,1)S(1)} %compare_reduce_fusion, f32[2,16]{0,1:T(8,128)S(1)} %copy.89, f32[2,16,64,128]{3,2,1,0:T(8,128)S(1)} %copy-done, s32[2]{0:T(128)S(1)} %fusion.46), kind=kOutput, calls=%fused_computation.42 | convolution fusion | flops 7077892 | bytes 4194442 | tf_op jit(solution)/shard_map/cr,rhpn->chpn/dot_general | solution.py:82
  101.3 0.8 collective-permute-start.5
  102.2 2.5 %collective-permute-start.3 = (f32[8]{0:T(128)S(1)}, f32[8]{0:T(128)S(1)}, u32[]{:S(2)}, u32[]{:S(2)}) collective-permute-start(f32[8]{0:T(128)S(1)} %get-tuple-element.18), channel_id=1, source_target_pairs={{0,16},{4,20},{8,24},{12,28},{16,32},{20,36},{24,40},{28,44},{32,4... | collective-permute-start | bytes 104 | tf_op jit(solution)/shard_map/ppermute | solution.py:17
  104.8 1.4 collective-permute-start.12
  106.2 2.1 %collective-permute-done.3 = f32[8]{0:T(128)S(1)} collective-permute-done((f32[8]{0:T(128)S(1)}, f32[8]{0:T(128)S(1)}, u32[]{:S(2)}, u32[]{:S(2)}) %collective-permute-start.3) | collective-permute-done | bytes 64 | tf_op jit(solution)/shard_map/ppermute | solution.py:17
  108.6 1.0 collective-permute-start.6
  109.6 1.3 collective-permute-done.12
  111.0 1.0 collective-permute-done.4
  112.0 1.6 collective-permute-start.10
  113.6 4.8 %collective-permute-done.6 = f32[8,64,128]{2,1,0:T(8,128)S(1)} collective-permute-done((f32[8,64,128]{2,1,0:T(8,128)S(1)}, f32[8,64,128]{2,1,0:T(8,128)S(1)}, u32[]{:S(2)}, u32[]{:S(2)}) %collective-permute-start.6) | collective-permute-done | bytes 262176 | tf_op jit(solution)/shard_map/ppermute | solution.py:17
  118.7 1.2 collective-permute-start.18
  119.8 4.0 %collective-permute-done.14 = f32[8,64,128]{2,1,0:T(8,128)S(1)} collective-permute-done((f32[8,64,128]{2,1,0:T(8,128)S(1)}, f32[8,64,128]{2,1,0:T(8,128)S(1)}, u32[]{:S(2)}, u32[]{:S(2)}) %collective-permute-start.14) | collective-permute-done | bytes 262176 | tf_op jit(solution)/shard_map/ppermute | solution.py:17
  124.2 4.8 %collective-permute-done.7 = f32[8,64,128]{2,1,0:T(8,128)S(1)} collective-permute-done((f32[8,64,128]{2,1,0:T(8,128)S(1)}, f32[8,64,128]{2,1,0:T(8,128)S(1)}, u32[]{:S(2)}, u32[]{:S(2)}) %collective-permute-start.7) | collective-permute-done | bytes 262176 | tf_op jit(solution)/shard_map/ppermute | solution.py:17
  129.3 5.3 %collective-permute-done.15 = f32[8,64,128]{2,1,0:T(8,128)S(1)} collective-permute-done((f32[8,64,128]{2,1,0:T(8,128)S(1)}, f32[8,64,128]{2,1,0:T(8,128)S(1)}, u32[]{:S(2)}, u32[]{:S(2)}) %collective-permute-start.15) | collective-permute-done | bytes 262176 | tf_op jit(solution)/shard_map/ppermute | solution.py:17
  134.8 0.8 collective-permute-done.8
  135.7 1.4 collective-permute-start.9
  137.3 5.9 %collective-permute-done.16 = f32[8,64,128]{2,1,0:T(8,128)S(1)} collective-permute-done((f32[8,64,128]{2,1,0:T(8,128)S(1)}, f32[8,64,128]{2,1,0:T(8,128)S(1)}, u32[]{:S(2)}, u32[]{:S(2)}) %collective-permute-start.16) | collective-permute-done | bytes 262176 | tf_op jit(solution)/shard_map/ppermute | solution.py:17
  143.7 3.7 %collective-permute-done.9 = f32[8,64,128]{2,1,0:T(8,128)S(1)} collective-permute-done((f32[8,64,128]{2,1,0:T(8,128)S(1)}, f32[8,64,128]{2,1,0:T(8,128)S(1)}, u32[]{:S(2)}, u32[]{:S(2)}) %collective-permute-start.9) | collective-permute-done | bytes 262176 | tf_op jit(solution)/shard_map/ppermute | solution.py:17
  147.7 5.8 %collective-permute-done.17 = f32[8,64,128]{2,1,0:T(8,128)S(1)} collective-permute-done((f32[8,64,128]{2,1,0:T(8,128)S(1)}, f32[8,64,128]{2,1,0:T(8,128)S(1)}, u32[]{:S(2)}, u32[]{:S(2)}) %collective-permute-start.17) | collective-permute-done | bytes 262176 | tf_op jit(solution)/shard_map/ppermute | solution.py:17
  153.9 1.1 bitcast_select_fusion.1
  155.1 10.9 %collective-permute-start.19 = (f32[16,64,128]{2,1,0:T(8,128)}, f32[16,64,128]{2,1,0:T(8,128)}, u32[]{:S(2)}, u32[]{:S(2)}) collective-permute-start(f32[16,64,128]{2,1,0:T(8,128)} %get-tuple-element.31), channel_id=1, source_target_pairs={{0,4},{4,0},{8,12},{12,8},{16,20},{20,16},{24,28},{28,24},{32,36},... | collective-permute-start | bytes 1572872 | tf_op jit(solution)/shard_map/ppermute | solution.py:175
  166.0 1.8 copy.98
  167.9 1.3 fusion.37
  169.2 1.4 copy.93
  170.6 1.4 copy.94
  172.1 0.8 fusion.24
  173.0 2.1 %fusion.25 = f32[2,16,64,256]{3,2,1,0:T(8,128)S(1)} fusion(f32[2,16,64,128]{3,0,2,1:T(2,128)S(1)} %fusion.24, bf16[2,256,1280]{2,1,0:T(8,128)(2,1)} %copy-done.1), kind=kOutput, calls=%fused_computation.40 | convolution fusion | flops 805306368 | bytes 3276800 | tf_op jit(solution)/shard_map/cqgn,cgjpn->cqgjp/dot_general | solution.py:184
  175.0 2.6 %fusion.19 = f32[2,256,1,16,64]{1,4,3,0,2:T(8,128)S(1)} fusion(f32[2,16,64,256]{3,2,1,0:T(8,128)S(1)} %fusion.25, f32[2,256,1,16,64]{1,4,3,0,2:T(8,128)S(1)} %bitcast.149, bf16[2,256,16,64]{1,3,2,0:T(8,128)(2,1)S(1)} %bitcast.147, f32[2,16,256]{2,1,0:T(8,128)S(1)} %get-tuple-element.42, f32[2,16,256]{2,1,0:T(8,128)S(1)} %get-tuple-element.45, ...), kind=kOutput, calls=%fused_computation.30 | convolution fusion | flops 281018368 | bytes 8028224 | tf_op jit(solution)/shard_map/cgjqk,ckgjp->cqgjp/dot_general | solution.py:109
  177.7 3.8 %copy.105 = f32[2,256,1,16,64]{4,3,1,0,2:T(8,128)} copy(f32[2,256,1,16,64]{1,4,3,0,2:T(8,128)S(1)} %fusion.19) | data formatting | bytes 4194304 | tf_op jit(solution)/shard_map/reshape | solution.py:193
  181.5 3.5 %reshape.290 = f32[512,1024]{1,0:T(8,128)S(1)} reshape(f32[2,256,1,16,64]{4,3,1,0,2:T(8,128)} %copy.105) | data formatting | bytes 4194304 | tf_op jit(solution)/shard_map/reshape | solution.py:193
  185.0 2.1 %multiply_reduce_fusion = f32[512]{0:T(512)S(1)} fusion(f32[512,1024]{1,0:T(8,128)S(1)} %reshape.290, bf16[512,2048]{1,0:T(8,128)(2,1)} %copy-done.2), kind=kLoop, calls=%fused_computation.32 | loop fusion | flops 4193792 | bytes 3147776 | tf_op jit(solution)/shard_map/reduce_sum | solution.py:195
  187.1 1.7 multiply_convert_fusion.3
  (132 shorter events, 6.7 us)
Async XLA Ops:
  6.5 90.0 %copy-start = (f32[2,16,64,128]{3,2,1,0:T(8,128)S(1)}, f32[2,16,64,128]{3,2,1,0:T(8,128)}, u32[]{:S(2)}) copy-start(f32[2,16,64,128]{3,2,1,0:T(8,128)} %param.30) | copy-start | bytes 3145732
  6.5 53.7 %all-gather.2.cloned.1.call-start = ((), (), s32[]{:S(2)}) async-start(), calls=%async_computation | async-start | bytes 5242880 | tf_op jit(solution)/shard_map/all_gather | solution.py:57
  8.4 17.2 %copy-start.13 = (bf16[2,3,2,128]{3,2,1,0:T(2,128)(2,1)S(1)}, bf16[2,3,2,128]{3,2,1,0:T(2,128)(2,1)}, u32[]{:S(2)}) copy-start(bf16[2,3,2,128]{3,2,1,0:T(2,128)(2,1)} %param.32) | copy-start | bytes 9220
  8.4 17.3 %copy-start.11 = (f32[1024]{0:T(1024)S(1)}, f32[1024]{0:T(1024)}, u32[]{:S(2)}) copy-start(f32[1024]{0:T(1024)} %param.23) | copy-start | bytes 12292
  8.4 17.3 %copy-start.15 = (f32[2,128]{1,0:T(2,128)S(1)}, f32[2,128]{1,0:T(2,128)}, u32[]{:S(2)}) copy-start(f32[2,128]{1,0:T(2,128)} %param.25) | copy-start | bytes 3076
  8.4 17.3 %copy-start.9 = (f32[4,1024]{1,0:T(4,128)S(1)}, f32[4,1024]{1,0:T(4,128)}, u32[]{:S(2)}) copy-start(f32[4,1024]{1,0:T(4,128)} %param.22) | copy-start | bytes 49156
  8.4 17.7 %copy-start.12 = (f32[4,2,128]{2,1,0:T(2,128)S(1)}, f32[4,2,128]{2,1,0:T(2,128)}, u32[]{:S(2)}) copy-start(f32[4,2,128]{2,1,0:T(2,128)} %param.24) | copy-start | bytes 12292
  8.4 17.8 %copy-start.18 = (f32[16]{0:T(128)S(1)}, f32[16]{0:T(128)}, u32[]{:S(2)}) copy-start(f32[16]{0:T(128)} %param.26) | copy-start | bytes 196
  60.3 15.9 %copy-start.4 = (bf16[512,4096]{1,0:T(8,128)(2,1)S(1)}, bf16[512,4096]{1,0:T(8,128)(2,1)}, u32[]{:S(2)}) copy-start(bf16[512,4096]{1,0:T(8,128)(2,1)} %all-gather.2.cloned.1.call-done) | copy-start | bytes 12582916
  76.0 3.7 %copy-start.2 = (bf16[512,2048]{1,0:T(8,128)(2,1)}, bf16[512,2048]{1,0:T(8,128)(2,1)S(1)}, u32[]{:S(2)}) copy-start(bf16[512,2048]{1,0:T(8,128)(2,1)S(1)} %convolution_convert_fusion) | copy-start | bytes 6291460
  76.1 2.4 %copy-start.16 = (bf16[4096,2,128]{2,1,0:T(2,128)(2,1)S(1)}, bf16[4096,2,128]{2,1,0:T(2,128)(2,1)}, u32[]{:S(2)}) copy-start(bf16[4096,2,128]{2,1,0:T(2,128)(2,1)} %param.20) | copy-start | bytes 6291460
  79.7 2.2 %copy-start.8 = (bf16[4096,16]{0,1:T(8,128)(2,1)S(1)}, bf16[4096,16]{0,1:T(8,128)(2,1)}, u32[]{:S(2)}) copy-start(bf16[4096,16]{0,1:T(8,128)(2,1)} %param.21) | copy-start | bytes 393220
  79.9 3.3 %copy-start.14 = (f32[16]{0:T(128)S(1)}, f32[16]{0:T(128)}, u32[]{:S(2)}) copy-start(f32[16]{0:T(128)} %param.27) | copy-start | bytes 196
  79.9 9.1 %copy-start.17 = (bf16[2,3,1024]{2,0,1:T(2,128)(2,1)S(1)}, bf16[2,3,1024]{2,0,1:T(2,128)(2,1)}, u32[]{:S(2)}) copy-start(bf16[2,3,1024]{2,0,1:T(2,128)(2,1)} %param.31) | copy-start | bytes 36868
  79.9 9.1 %collective-permute-start = (bf16[2,3,1280]{2,0,1:T(2,128)(2,1)S(1)}, bf16[2,3,1280]{2,0,1:T(2,128)(2,1)S(1)}, u32[]{:S(2)}, u32[]{:S(2)}) collective-permute-start(bf16[2,3,1280]{2,0,1:T(2,128)(2,1)S(1)} %copy.107), channel_id=1, source_target_pairs={{0,4},{4,8},{8,12},{12,16},{16,20},{20,24},{24,28},{28,32},{32,36}... | collective-permute-start | bytes 46088 | tf_op jit(solution)/shard_map/ppermute | solution.py:17
  85.3 1.2 collective-permute-start.1
  86.7 15.5 %collective-permute-start.2 = (f32[8]{0:T(128)S(1)}, f32[8]{0:T(128)S(1)}, u32[]{:S(2)}, u32[]{:S(2)}) collective-permute-start(f32[8]{0:T(128)S(1)} %reshape_squeeze.12), channel_id=1, source_target_pairs={{0,8},{4,12},{8,16},{12,20},{16,24},{20,28},{24,32},{28,36},{32,40... | collective-permute-start | bytes 104 | tf_op jit(solution)/shard_map/ppermute | solution.py:17
  88.0 16.7 %collective-permute-start.11 = (f32[8]{0:T(128)S(1)}, f32[8]{0:T(128)S(1)}, u32[]{:S(2)}, u32[]{:S(2)}) collective-permute-start(f32[8]{0:T(128)S(1)} %reshape_squeeze.14), channel_id=1, source_target_pairs={{0,8},{4,12},{8,16},{12,20},{16,24},{20,28},{24,32},{28,36},{32,40... | collective-permute-start | bytes 104 | tf_op jit(solution)/shard_map/ppermute | solution.py:17
  91.2 1.4 copy-start.1
  101.3 7.1 %collective-permute-start.5 = (f32[16,64,128]{2,1,0:T(8,128)S(1)}, f32[16,64,128]{2,1,0:T(8,128)S(1)}, u32[]{:S(2)}, u32[]{:S(2)}) collective-permute-start(f32[16,64,128]{2,1,0:T(8,128)S(1)} %bitcast.155), channel_id=1, source_target_pairs={{0,4},{4,0},{8,12},{12,8},{16,20},{20,16},{24,28},{28,24},{32,36},... | collective-permute-start | bytes 1572872 | tf_op jit(solution)/shard_map/ppermute | solution.py:133
  102.2 6.0 %collective-permute-start.3 = (f32[8]{0:T(128)S(1)}, f32[8]{0:T(128)S(1)}, u32[]{:S(2)}, u32[]{:S(2)}) collective-permute-start(f32[8]{0:T(128)S(1)} %get-tuple-element.18), channel_id=1, source_target_pairs={{0,16},{4,20},{8,24},{12,28},{16,32},{20,36},{24,40},{28,44},{32,4... | collective-permute-start | bytes 104 | tf_op jit(solution)/shard_map/ppermute | solution.py:17
  104.8 6.0 %collective-permute-start.12 = (f32[8]{0:T(128)S(1)}, f32[8]{0:T(128)S(1)}, u32[]{:S(2)}, u32[]{:S(2)}) collective-permute-start(f32[8]{0:T(128)S(1)} %get-tuple-element.25), channel_id=1, source_target_pairs={{0,16},{4,20},{8,24},{12,28},{16,32},{20,36},{24,40},{28,44},{32,4... | collective-permute-start | bytes 104 | tf_op jit(solution)/shard_map/ppermute | solution.py:17
  108.3 3.6 %collective-permute-start.4 = (f32[8]{0:T(128)S(1)}, f32[8]{0:T(128)S(1)}, u32[]{:S(2)}, u32[]{:S(2)}) collective-permute-start(f32[8]{0:T(128)S(1)} %fusion.58), channel_id=1, source_target_pairs={{0,32},{4,36},{8,40},{12,44},{16,48},{20,52},{24,56},{28,60},{32,6... | collective-permute-start | bytes 104 | tf_op jit(solution)/shard_map/ppermute | solution.py:17
  108.6 9.8 %collective-permute-start.6 = (f32[8,64,128]{2,1,0:T(8,128)S(1)}, f32[8,64,128]{2,1,0:T(8,128)S(1)}, u32[]{:S(2)}, u32[]{:S(2)}) collective-permute-start(f32[8,64,128]{2,1,0:T(8,128)S(1)} %bitcast.154), channel_id=1, source_target_pairs={{0,8},{4,12},{8,16},{12,20},{16,24},{20,28},{24,32},{28,36},{32,40... | collective-permute-start | bytes 786440 | tf_op jit(solution)/shard_map/ppermute | solution.py:17
  110.9 7.7 %collective-permute-start.13 = (f32[8]{0:T(128)S(1)}, f32[8]{0:T(128)S(1)}, u32[]{:S(2)}, u32[]{:S(2)}) collective-permute-start(f32[8]{0:T(128)S(1)} %fusion.60), channel_id=1, source_target_pairs={{0,32},{4,36},{8,40},{12,44},{16,48},{20,52},{24,56},{28,60},{32,6... | collective-permute-start | bytes 104 | tf_op jit(solution)/shard_map/ppermute | solution.py:17
  112.0 17.1 %collective-permute-start.10 = (f32[8]{0:T(128)S(1)}, f32[8]{0:T(128)S(1)}, u32[]{:S(2)}, u32[]{:S(2)}) collective-permute-start(f32[8]{0:T(128)S(1)} %fusion.53), channel_id=1, source_target_pairs={{0,64},{4,68},{8,72},{12,76},{16,80},{20,84},{24,88},{28,92},{32,9... | collective-permute-start | bytes 104 | tf_op jit(solution)/shard_map/ppermute | solution.py:17
  113.6 10.3 %collective-permute-start.14 = (f32[8,64,128]{2,1,0:T(8,128)S(1)}, f32[8,64,128]{2,1,0:T(8,128)S(1)}, u32[]{:S(2)}, u32[]{:S(2)}) collective-permute-start(f32[8,64,128]{2,1,0:T(8,128)S(1)} %bitcast.153), channel_id=1, source_target_pairs={{0,8},{4,12},{8,16},{12,20},{16,24},{20,28},{24,32},{28,36},{32,40... | collective-permute-start | bytes 786440 | tf_op jit(solution)/shard_map/ppermute | solution.py:17
  118.5 10.5 %collective-permute-start.7 = (f32[8,64,128]{2,1,0:T(8,128)S(1)}, f32[8,64,128]{2,1,0:T(8,128)S(1)}, u32[]{:S(2)}, u32[]{:S(2)}) collective-permute-start(f32[8,64,128]{2,1,0:T(8,128)S(1)} %multiply_add_fusion.5), channel_id=1, source_target_pairs={{0,16},{4,20},{8,24},{12,28},{16,32},{20,36},{24,40},{28,44},{32,4... | collective-permute-start | bytes 786440 | tf_op jit(solution)/shard_map/ppermute | solution.py:17
  118.7 18.4 %collective-permute-start.18 = (f32[8]{0:T(128)S(1)}, f32[8]{0:T(128)S(1)}, u32[]{:S(2)}, u32[]{:S(2)}) collective-permute-start(f32[8]{0:T(128)S(1)} %fusion.55), channel_id=1, source_target_pairs={{0,64},{4,68},{8,72},{12,76},{16,80},{20,84},{24,88},{28,92},{32,9... | collective-permute-start | bytes 104 | tf_op jit(solution)/shard_map/ppermute | solution.py:17
  124.0 10.6 %collective-permute-start.15 = (f32[8,64,128]{2,1,0:T(8,128)S(1)}, f32[8,64,128]{2,1,0:T(8,128)S(1)}, u32[]{:S(2)}, u32[]{:S(2)}) collective-permute-start(f32[8,64,128]{2,1,0:T(8,128)S(1)} %multiply_add_fusion.2), channel_id=1, source_target_pairs={{0,16},{4,20},{8,24},{12,28},{16,32},{20,36},{24,40},{28,44},{32,4... | collective-permute-start | bytes 786440 | tf_op jit(solution)/shard_map/ppermute | solution.py:17
  129.1 6.5 %collective-permute-start.8 = (f32[8,64,128]{2,1,0:T(8,128)S(1)}, f32[8,64,128]{2,1,0:T(8,128)S(1)}, u32[]{:S(2)}, u32[]{:S(2)}) collective-permute-start(f32[8,64,128]{2,1,0:T(8,128)S(1)} %multiply_add_fusion.4), channel_id=1, source_target_pairs={{0,32},{4,36},{8,40},{12,44},{16,48},{20,52},{24,56},{28,60},{32,6... | collective-permute-start | bytes 786440 | tf_op jit(solution)/shard_map/ppermute | solution.py:17
  134.7 8.6 %collective-permute-start.16 = (f32[8,64,128]{2,1,0:T(8,128)S(1)}, f32[8,64,128]{2,1,0:T(8,128)S(1)}, u32[]{:S(2)}, u32[]{:S(2)}) collective-permute-start(f32[8,64,128]{2,1,0:T(8,128)S(1)} %multiply_add_fusion.1), channel_id=1, source_target_pairs={{0,32},{4,36},{8,40},{12,44},{16,48},{20,52},{24,56},{28,60},{32,6... | collective-permute-start | bytes 786440 | tf_op jit(solution)/shard_map/ppermute | solution.py:17
  135.7 11.7 %collective-permute-start.9 = (f32[8,64,128]{2,1,0:T(8,128)S(1)}, f32[8,64,128]{2,1,0:T(8,128)S(1)}, u32[]{:S(2)}, u32[]{:S(2)}) collective-permute-start(f32[8,64,128]{2,1,0:T(8,128)S(1)} %multiply_add_fusion.3), channel_id=1, source_target_pairs={{0,64},{4,68},{8,72},{12,76},{16,80},{20,84},{24,88},{28,92},{32,9... | collective-permute-start | bytes 786440 | tf_op jit(solution)/shard_map/ppermute | solution.py:17
  143.4 10.2 %collective-permute-start.17 = (f32[8,64,128]{2,1,0:T(8,128)S(1)}, f32[8,64,128]{2,1,0:T(8,128)S(1)}, u32[]{:S(2)}, u32[]{:S(2)}) collective-permute-start(f32[8,64,128]{2,1,0:T(8,128)S(1)} %multiply_add_fusion), channel_id=1, source_target_pairs={{0,64},{4,68},{8,72},{12,76},{16,80},{20,84},{24,88},{28,92},{32,9... | collective-permute-start | bytes 786440 | tf_op jit(solution)/shard_map/ppermute | solution.py:17
  155.1 15.5 %collective-permute-start.19 = (f32[16,64,128]{2,1,0:T(8,128)}, f32[16,64,128]{2,1,0:T(8,128)}, u32[]{:S(2)}, u32[]{:S(2)}) collective-permute-start(f32[16,64,128]{2,1,0:T(8,128)} %get-tuple-element.31), channel_id=1, source_target_pairs={{0,4},{4,0},{8,12},{12,8},{16,20},{20,16},{24,28},{28,24},{32,36},... | collective-permute-start | bytes 1572872 | tf_op jit(solution)/shard_map/ppermute | solution.py:175
  167.9 4.2 %copy-start.7 = (f32[2,16,64,128]{3,0,2,1:T(2,128)S(1)}, f32[2,16,64,128]{3,0,2,1:T(2,128)}, u32[]{:S(2)}) copy-start(f32[2,16,64,128]{3,0,2,1:T(2,128)} %get-tuple-element.52) | copy-start | bytes 3145732
  172.9 2.1 %copy-start.5 = (bf16[2,256,1024]{1,2,0:T(8,128)(2,1)S(1)}, bf16[2,256,1024]{1,2,0:T(8,128)(2,1)}, u32[]{:S(2)}) copy-start(bf16[2,256,1024]{1,2,0:T(8,128)(2,1)} %copy.84) | copy-start | bytes 3145732
  172.9 2.1 %copy-start.6 = (f32[2,256,1024]{1,2,0:T(8,128)S(1)}, f32[2,256,1024]{1,2,0:T(8,128)}, u32[]{:S(2)}) copy-start(f32[2,256,1024]{1,2,0:T(8,128)} %copy.98) | copy-start | bytes 6291460
  172.9 2.1 %copy-start.19 = (f32[16]{0:T(128)S(1)}, f32[16]{0:T(128)}, u32[]{:S(2)}) copy-start(f32[16]{0:T(128)} %param.28) | copy-start | bytes 196
  185.0 2.1 %copy-start.3 = (bf16[512,2048]{1,0:T(8,128)(2,1)S(1)}, bf16[512,2048]{1,0:T(8,128)(2,1)}, u32[]{:S(2)}) copy-start(bf16[512,2048]{1,0:T(8,128)(2,1)} %copy-done.2) | copy-start | bytes 6291460
  185.0 2.1 %copy-start.10 = (f32[1024]{0:T(1024)S(1)}, f32[1024]{0:T(1024)}, u32[]{:S(2)}) copy-start(f32[1024]{0:T(1024)} %param.29) | copy-start | bytes 12292
Sparse Core Ops, SparseCore 0:
  9.0 51.2 all-gather.1
where the time goes:
time: 196 us
  waiting for transfers between devices  75.5 us (39%)
  local copies, waits for them, and re-layouts  35.3 us (18%)
  matrix products  30.7 us (16%)
  starting transfers between devices  25.8 us (13%)
  other arithmetic  14.2 us (7%)
  between operations  14.1 us (7%)
    ppermute x17, waiting for transfers between devices, from_behind(): return lax.ppermute(value, axis, pairs)  39.6 us
    all_gather x1, waiting for transfers between devices, per_device(): piece = lax.all_gather(hidden, 'mp', axis=1, tiled=True)  34.1 us
    unnamed x44, local copies, waits for them, and re-layouts  19.5 us
    dot_general x1, matrix products, per_device(): zx_sum = jnp.dot(piece, flat_zx, preferred_element_type=jnp.float32)  15.8 us
    ppermute x17, starting transfers between devices, from_behind(): return lax.ppermute(value, axis, pairs)  14.1 us
    ppermute x1, starting transfers between devices, per_device(): lax.ppermute(jnp.where(core == 0, after_early, before_chip), 'seq', pair)  10.9 us
    reshape x2, local copies, waits for them, and re-layouts, per_device(): y_total.reshape(rows_dev, inner_dev) * jax.nn.silu(gate.astype(jnp.float32))  7.29 us
    dot_general x1, matrix products, per_device(): jnp.einsum('cr,rhpn->chpn', pick, state_bank, precision=lax.Precision.HIG...  4.63 us
  transfers between devices with their start and end apart: 21, of which 13 were waited for; matrix products, arithmetic and copies ran while one was open for 21% of the time, Pallas kernels for 0%

commit v1 on v0

--- a/solution.py
+++ b/solution.py
@@ -9,6 +9,24 @@
 BLOCK = 256
 KERNEL = 4
 BANK = 2
+
+
+def gather_around(value, axis, dim):
+    ways, here, step = (lax.axis_size(axis), lax.axis_index(axis), value.shape[dim])
+    lengths = [n * ways if d == dim else n for d, n in enumerate(value.shape)]
+    full = lax.dynamic_update_slice_in_dim(
+        jnp.zeros(lengths, value.dtype), value, here * step, axis=dim
+    )
+    going_up = going_down = value
+    for far in range(1, ways // 2 + 1):
+        going_up = lax.ppermute(going_up, axis, [(d, (d + 1) % ways) for d in range(ways)])
+        full = lax.dynamic_update_slice_in_dim(full, going_up, (here - far) % ways * step, axis=dim)
+        if 2 * far < ways:
+            going_down = lax.ppermute(going_down, axis, [(d, (d - 1) % ways) for d in range(ways)])
+            full = lax.dynamic_update_slice_in_dim(
+                full, going_down, (here + far) % ways * step, axis=dim
+            )
+    return full
 
 
 def from_behind(value, axis, steps):
@@ -54,7 +72,7 @@
     prompts = prompt_blocks.shape[0]
     flat_zx = w_zx.reshape(WIDTH, 2 * inner_dev)
     flat_bc = w_bc.reshape(WIDTH, 2 * gstate_dev)
-    piece = lax.all_gather(hidden, "mp", axis=1, tiled=True)
+    piece = gather_around(hidden, "mp", 1)
     zx_sum = jnp.dot(piece, flat_zx, preferred_element_type=jnp.float32)
     bc_sum = jnp.dot(piece, flat_bc, preferred_element_type=jnp.float32)
     dt_raw = jnp.dot(piece, w_dt, preferred_element_type=jnp.float32)

time: 196 us -> 184 us (0.939)
  between operations: 14.1 us -> 0.77 us
  waiting for transfers between devices: 75.5 us -> 71.6 us
  local copies, waits for them, and re-layouts: 35.3 us -> 38.3 us
  starting transfers between devices: 25.8 us -> 28.1 us
    all_gather x1 -> x0, waiting for transfers between devices: 34.1 us -> none  [per_device(): piece = lax.all_gather(hidden, 'mp', axis=1, tiled=True)]
    ppermute x0 -> x3, waiting for transfers between devices: none -> 26.4 us  [the longest x2 26.4 us: gather_around(): lax.ppermute(going_up, axis, [(d, (d + 1) % ways) for d in range(ways)])]
    ppermute x17, waiting for transfers between devices: 39.6 us -> 45.1 us  [from_behind(): return lax.ppermute(value, axis, pairs)]
    ppermute x17, starting transfers between devices: 14.1 us -> 9.03 us  [from_behind(): return lax.ppermute(value, axis, pairs)]
    ppermute x2, starting transfers between devices: 0.8 us -> 5.2 us  [per_device(): lax.ppermute((keep(step_a, 1 - core), keep(step_b, 1 - core)), 'seq', pair)]
    ppermute x0 -> x3, starting transfers between devices: none -> 3.63 us  [the longest x2 2.12 us: gather_around(): lax.ppermute(going_up, axis, [(d, (d + 1) % ways) for d in range(ways)])]
    unnamed x44 -> x48, local copies, waits for them, and re-layouts: 19.5 us -> 20.2 us
  transfers between devices with their start and end apart: 21 -> 23, of which waited for: 13 -> 12; matrix products, arithmetic and copies ran while one was open for 21% -> 31% of each run, Pallas kernels for 0% -> 0%
where the time goes in v1:
time: 184 us; the launch traced here: 183 us
  waiting for transfers between devices  71.6 us (39%)
  local copies, waits for them, and re-layouts  38.3 us (21%)
  matrix products  30.6 us (17%)
  starting transfers between devices  28.1 us (15%)
  other arithmetic  14.1 us (8%)
    ppermute x17, waiting for transfers between devices, from_behind(): return lax.ppermute(value, axis, pairs)  45.1 us
    ppermute x2, waiting for transfers between devices, gather_around(): lax.ppermute(going_up, axis, [(d, (d + 1) % ways) for d in range(ways)])  26.4 us
    unnamed x48, local copies, waits for them, and re-layouts  20.2 us
    dot_general x1, matrix products, per_device(): zx_sum = jnp.dot(piece, flat_zx, preferred_element_type=jnp.float32)  15.7 us
    ppermute x1, starting transfers between devices, per_device(): lax.ppermute(jnp.where(core == 0, after_early, before_chip), 'seq', pair)  10.2 us
    ppermute x17, starting transfers between devices, from_behind(): return lax.ppermute(value, axis, pairs)  9.03 us
    reshape x2, local copies, waits for them, and re-layouts, per_device(): y_total.reshape(rows_dev, inner_dev) * jax.nn.silu(gate.astype(jnp.float32))  7.28 us
    ppermute x2, starting transfers between devices, per_device(): lax.ppermute((keep(step_a, 1 - core), keep(step_b, 1 - core)), 'seq', pair)  5.2 us
  transfers between devices with their start and end apart: 23, of which 12 were waited for; matrix products, arithmetic and copies ran while one was open for 31% of the time, Pallas kernels for 0%

profile of v1, /device:TPU:1, one launch (start us, length us, event | category | flops | bytes accessed | tf_op | source)
XLA Modules:
  0.0 183.4 jit_solution(14752957720986038420)
XLA Ops:
  0.0 2.1 %collective-permute-start = (bf16[512,1024]{1,0:T(8,128)(2,1)}, bf16[512,1024]{1,0:T(8,128)(2,1)S(1)}, u32[]{:S(2)}, u32[]{:S(2)}) collective-permute-start(bf16[512,1024]{1,0:T(8,128)(2,1)} %param.18), channel_id=1, source_target_pairs={{0,1},{1,2},{2,3},{3,0},{4,5},{5,6},{6,7},{7,4},{8,9},{9,10},{10,1... | collective-permute-start | bytes 3145736 | tf_op jit(solution)/shard_map/ppermute | solution.py:22
  2.1 1.5 collective-permute-start.1
  3.6 0.9 select_reduce_fusion.1
  4.7 17.1 %copy.111 = bf16[512,8,2,1024]{3,1,2,0:T(8,128)(2,1)} copy(bf16[512,8,2,1024]{3,2,1,0:T(2,128)(2,1)} %bitcast.142) | data formatting | bytes 33554432
  22.3 4.2 %collective-permute-done = bf16[512,1024]{1,0:T(8,128)(2,1)S(1)} collective-permute-done((bf16[512,1024]{1,0:T(8,128)(2,1)}, bf16[512,1024]{1,0:T(8,128)(2,1)S(1)}, u32[]{:S(2)}, u32[]{:S(2)}) %collective-permute-start) | collective-permute-done | bytes 1048608 | tf_op jit(solution)/shard_map/ppermute | solution.py:22
  27.5 1.4 constant_dynamic-update-slice_fusion.3
  28.9 22.2 %collective-permute-done.2 = bf16[512,1024]{1,0:T(8,128)(2,1)S(1)} collective-permute-done((bf16[512,1024]{1,0:T(8,128)(2,1)S(1)}, bf16[512,1024]{1,0:T(8,128)(2,1)S(1)}, u32[]{:S(2)}, u32[]{:S(2)}) %collective-permute-start.2) | collective-permute-done | bytes 1048608 | tf_op jit(solution)/shard_map/ppermute | solution.py:22
  51.2 1.9 %copy-done.1 = bf16[512,4096]{1,0:T(8,128)(2,1)} copy-done((bf16[512,4096]{1,0:T(8,128)(2,1)}, bf16[512,4096]{1,0:T(8,128)(2,1)S(1)}, u32[]{:S(2)}) %copy-start.1) | copy-done | bytes 4194328
  53.2 1.2 fusion.73
  54.5 1.2 reduce-window.18
  56.4 2.2 %collective-permute-start.4 = (f32[16]{0:T(128)S(1)}, f32[16]{0:T(128)S(1)}, u32[]{:S(2)}, u32[]{:S(2)}) collective-permute-start(f32[16]{0:T(128)S(1)} %reshape.274), channel_id=1, source_target_pairs={{0,4},{4,0},{8,12},{12,8},{16,20},{20,16},{24,28},{28,24},{32,36},... | collective-permute-start | bytes 200 | tf_op jit(solution)/shard_map/ppermute | solution.py:151
  58.7 15.7 %convolution_convert_fusion = bf16[512,2048]{1,0:T(8,128)(2,1)S(1)} fusion(bf16[512,4096]{1,0:T(8,128)(2,1)} %copy-done.1, bf16[4096,2048]{1,0:T(8,128)(2,1)} %bitcast.143), kind=kOutput, calls=%fused_computation.8 | convolution fusion | flops 8590983168 | bytes 23068672 | tf_op jit(solution)/shard_map/dot_general | solution.py:76
  74.6 1.3 fusion.20
  76.0 1.5 collective-permute-start.3
  77.8 1.6 collective-permute-start.5
  79.5 1.3 collective-permute-start.14
  81.4 1.7 multiply_convert_fusion.2
  83.1 1.1 copy-done.3
  84.2 1.3 slice_convert_fusion
  85.5 2.3 %copy.84 = bf16[2,256,1024]{1,2,0:T(8,128)(2,1)} copy(bf16[2,256,1024]{2,1,0:T(8,128)(2,1)} %get-tuple-element.33) | data formatting | bytes 2097152 | tf_op jit(solution)/shard_map/slice | solution.py:113
  87.7 1.7 fusion.23
  89.4 4.6 %copy_add_fusion = (f32[2,16,64,128]{3,0,2,1:T(2,128)S(1)}, f32[2,16,64,128]{3,0,2,1:T(2,128)}) fusion(f32[2,16,64,128]{3,2,1,0:T(8,128)S(1)} %fusion.23, pred[2]{0:T(512)(128)(4,1)S(1)} %compare_reduce_fusion, f32[2,16]{0,1:T(8,128)S(1)} %copy.89, f32[2,16,64,128]{3,2,1,0:T(8,128)S(1)} %copy-done, s32[2]{0:T(128)S(1)} %fusion.46), kind=kOutput, calls=%fused_computation.42 | convolution fusion | flops 7077892 | bytes 4194442 | tf_op jit(solution)/shard_map/cr,rhpn->chpn/dot_general | solution.py:100
  94.2 3.0 %collective-permute-start.8 = (f32[16,64,128]{2,1,0:T(8,128)S(1)}, f32[16,64,128]{2,1,0:T(8,128)S(1)}, u32[]{:S(2)}, u32[]{:S(2)}) collective-permute-start(f32[16,64,128]{2,1,0:T(8,128)S(1)} %bitcast.155), channel_id=1, source_target_pairs={{0,4},{4,0},{8,12},{12,8},{16,20},{20,16},{24,28},{28,24},{32,36},... | collective-permute-start | bytes 1572872 | tf_op jit(solution)/shard_map/ppermute | solution.py:151
  97.4 1.7 collective-permute-start.15
  99.0 4.3 %collective-permute-done.6 = f32[8]{0:T(128)S(1)} collective-permute-done((f32[8]{0:T(128)S(1)}, f32[8]{0:T(128)S(1)}, u32[]{:S(2)}, u32[]{:S(2)}) %collective-permute-start.6) | collective-permute-done | bytes 64 | tf_op jit(solution)/shard_map/ppermute | solution.py:35
  103.8 3.2 %collective-permute-done.7 = f32[8]{0:T(128)S(1)} collective-permute-done((f32[8]{0:T(128)S(1)}, f32[8]{0:T(128)S(1)}, u32[]{:S(2)}, u32[]{:S(2)}) %collective-permute-start.7) | collective-permute-done | bytes 64 | tf_op jit(solution)/shard_map/ppermute | solution.py:35
  107.7 6.0 %collective-permute-done.9 = f32[8,64,128]{2,1,0:T(8,128)S(1)} collective-permute-done((f32[8,64,128]{2,1,0:T(8,128)S(1)}, f32[8,64,128]{2,1,0:T(8,128)S(1)}, u32[]{:S(2)}, u32[]{:S(2)}) %collective-permute-start.9) | collective-permute-done | bytes 262176 | tf_op jit(solution)/shard_map/ppermute | solution.py:35
  114.0 5.4 %collective-permute-done.17 = f32[8,64,128]{2,1,0:T(8,128)S(1)} collective-permute-done((f32[8,64,128]{2,1,0:T(8,128)S(1)}, f32[8,64,128]{2,1,0:T(8,128)S(1)}, u32[]{:S(2)}, u32[]{:S(2)}) %collective-permute-start.17) | collective-permute-done | bytes 262176 | tf_op jit(solution)/shard_map/ppermute | solution.py:35
  119.6 4.3 %collective-permute-done.10 = f32[8,64,128]{2,1,0:T(8,128)S(1)} collective-permute-done((f32[8,64,128]{2,1,0:T(8,128)S(1)}, f32[8,64,128]{2,1,0:T(8,128)S(1)}, u32[]{:S(2)}, u32[]{:S(2)}) %collective-permute-start.10) | collective-permute-done | bytes 262176 | tf_op jit(solution)/shard_map/ppermute | solution.py:35
  124.2 5.4 %collective-permute-done.18 = f32[8,64,128]{2,1,0:T(8,128)S(1)} collective-permute-done((f32[8,64,128]{2,1,0:T(8,128)S(1)}, f32[8,64,128]{2,1,0:T(8,128)S(1)}, u32[]{:S(2)}, u32[]{:S(2)}) %collective-permute-start.18) | collective-permute-done | bytes 262176 | tf_op jit(solution)/shard_map/ppermute | solution.py:35
  129.8 0.7 collective-permute-done.11
  130.6 1.5 collective-permute-start.12
  132.3 6.4 %collective-permute-done.19 = f32[8,64,128]{2,1,0:T(8,128)S(1)} collective-permute-done((f32[8,64,128]{2,1,0:T(8,128)S(1)}, f32[8,64,128]{2,1,0:T(8,128)S(1)}, u32[]{:S(2)}, u32[]{:S(2)}) %collective-permute-start.19) | collective-permute-done | bytes 262176 | tf_op jit(solution)/shard_map/ppermute | solution.py:35
  139.1 3.3 %collective-permute-done.12 = f32[8,64,128]{2,1,0:T(8,128)S(1)} collective-permute-done((f32[8,64,128]{2,1,0:T(8,128)S(1)}, f32[8,64,128]{2,1,0:T(8,128)S(1)}, u32[]{:S(2)}, u32[]{:S(2)}) %collective-permute-start.12) | collective-permute-done | bytes 262176 | tf_op jit(solution)/shard_map/ppermute | solution.py:35
  142.8 6.2 %collective-permute-done.20 = f32[8,64,128]{2,1,0:T(8,128)S(1)} collective-permute-done((f32[8,64,128]{2,1,0:T(8,128)S(1)}, f32[8,64,128]{2,1,0:T(8,128)S(1)}, u32[]{:S(2)}, u32[]{:S(2)}) %collective-permute-start.20) | collective-permute-done | bytes 262176 | tf_op jit(solution)/shard_map/ppermute | solution.py:35
  149.3 1.2 bitcast_select_fusion.1
  150.5 10.2 %collective-permute-start.22 = (f32[16,64,128]{2,1,0:T(8,128)}, f32[16,64,128]{2,1,0:T(8,128)}, u32[]{:S(2)}, u32[]{:S(2)}) collective-permute-start(f32[16,64,128]{2,1,0:T(8,128)} %get-tuple-element.31), channel_id=1, source_target_pairs={{0,4},{4,0},{8,12},{12,8},{16,20},{20,16},{24,28},{28,24},{32,36},... | collective-permute-start | bytes 1572872 | tf_op jit(solution)/shard_map/ppermute | solution.py:193
  160.7 1.8 %copy.98 = f32[2,256,1024]{1,2,0:T(8,128)} copy(f32[2,256,1024]{2,1,0:T(8,128)S(1)} %get-tuple-element.32) | data formatting | bytes 4194304 | tf_op jit(solution)/shard_map/convert_element_type | solution.py:131
  162.6 1.3 fusion.37
  163.9 1.4 copy.93
  165.3 1.4 copy.94
  166.8 0.8 fusion.24
  167.7 2.0 %fusion.25 = f32[2,16,64,256]{3,2,1,0:T(8,128)S(1)} fusion(f32[2,16,64,128]{3,0,2,1:T(2,128)S(1)} %fusion.24, bf16[2,256,1280]{2,1,0:T(8,128)(2,1)} %copy-done.3), kind=kOutput, calls=%fused_computation.40 | convolution fusion | flops 805306368 | bytes 3276800 | tf_op jit(solution)/shard_map/cqgn,cgjpn->cqgjp/dot_general | solution.py:202
  169.7 2.6 %fusion.19 = f32[2,256,1,16,64]{1,4,3,0,2:T(8,128)S(1)} fusion(f32[2,16,64,256]{3,2,1,0:T(8,128)S(1)} %fusion.25, f32[2,256,1,16,64]{1,4,3,0,2:T(8,128)S(1)} %bitcast.149, bf16[2,256,16,64]{1,3,2,0:T(8,128)(2,1)S(1)} %bitcast.147, f32[2,16,256]{2,1,0:T(8,128)S(1)} %get-tuple-element.42, f32[2,16,256]{2,1,0:T(8,128)S(1)} %get-tuple-element.45, ...), kind=kOutput, calls=%fused_computation.30 | convolution fusion | flops 281018368 | bytes 8028224 | tf_op jit(solution)/shard_map/cgjqk,ckgjp->cqgjp/dot_general | solution.py:127
  172.3 3.8 %copy.105 = f32[2,256,1,16,64]{4,3,1,0,2:T(8,128)} copy(f32[2,256,1,16,64]{1,4,3,0,2:T(8,128)S(1)} %fusion.19) | data formatting | bytes 4194304 | tf_op jit(solution)/shard_map/reshape | solution.py:211
  176.1 3.5 %reshape.290 = f32[512,1024]{1,0:T(8,128)S(1)} reshape(f32[2,256,1,16,64]{4,3,1,0,2:T(8,128)} %copy.105) | data formatting | bytes 4194304 | tf_op jit(solution)/shard_map/reshape | solution.py:211
  179.6 2.1 %multiply_reduce_fusion = f32[512]{0:T(512)S(1)} fusion(f32[512,1024]{1,0:T(8,128)S(1)} %reshape.290, bf16[512,2048]{1,0:T(8,128)(2,1)} %copy-done.4), kind=kLoop, calls=%fused_computation.32 | loop fusion | flops 4193792 | bytes 3147776 | tf_op jit(solution)/shard_map/reduce_sum | solution.py:213
  181.7 1.7 multiply_convert_fusion.3
  (144 shorter events, 7.5 us)
Async XLA Ops:
  0.0 89.4 %copy-start = (f32[2,16,64,128]{3,2,1,0:T(8,128)S(1)}, f32[2,16,64,128]{3,2,1,0:T(8,128)}, u32[]{:S(2)}) copy-start(f32[2,16,64,128]{3,2,1,0:T(8,128)} %param.30) | copy-start | bytes 3145732
  0.0 26.5 %collective-permute-start = (bf16[512,1024]{1,0:T(8,128)(2,1)}, bf16[512,1024]{1,0:T(8,128)(2,1)S(1)}, u32[]{:S(2)}, u32[]{:S(2)}) collective-permute-start(bf16[512,1024]{1,0:T(8,128)(2,1)} %param.18), channel_id=1, source_target_pairs={{0,1},{1,2},{2,3},{3,0},{4,5},{5,6},{6,7},{7,4},{8,9},{9,10},{10,1... | collective-permute-start | bytes 3145736 | tf_op jit(solution)/shard_map/ppermute | solution.py:22
  2.1 25.3 %collective-permute-start.1 = (bf16[512,1024]{1,0:T(8,128)(2,1)}, bf16[512,1024]{1,0:T(8,128)(2,1)}, u32[]{:S(2)}, u32[]{:S(2)}) collective-permute-start(bf16[512,1024]{1,0:T(8,128)(2,1)} %param.18), channel_id=1, source_target_pairs={{0,3},{1,0},{2,1},{3,2},{4,7},{5,4},{6,5},{7,6},{8,11},{9,8},{10,9... | collective-permute-start | bytes 3145736 | tf_op jit(solution)/shard_map/ppermute | solution.py:25
  4.7 17.1 %copy-start.15 = (bf16[2,3,2,128]{3,2,1,0:T(2,128)(2,1)S(1)}, bf16[2,3,2,128]{3,2,1,0:T(2,128)(2,1)}, u32[]{:S(2)}) copy-start(bf16[2,3,2,128]{3,2,1,0:T(2,128)(2,1)} %param.32) | copy-start | bytes 9220
  4.7 17.6 %copy-start.11 = (f32[4,1024]{1,0:T(4,128)S(1)}, f32[4,1024]{1,0:T(4,128)}, u32[]{:S(2)}) copy-start(f32[4,1024]{1,0:T(4,128)} %param.22) | copy-start | bytes 49156
  4.7 21.8 %copy-start.13 = (f32[1024]{0:T(1024)S(1)}, f32[1024]{0:T(1024)}, u32[]{:S(2)}) copy-start(f32[1024]{0:T(1024)} %param.23) | copy-start | bytes 12292
  4.7 21.8 %copy-start.17 = (f32[2,128]{1,0:T(2,128)S(1)}, f32[2,128]{1,0:T(2,128)}, u32[]{:S(2)}) copy-start(f32[2,128]{1,0:T(2,128)} %param.25) | copy-start | bytes 3076
  4.7 21.8 %copy-start.14 = (f32[4,2,128]{2,1,0:T(2,128)S(1)}, f32[4,2,128]{2,1,0:T(2,128)}, u32[]{:S(2)}) copy-start(f32[4,2,128]{2,1,0:T(2,128)} %param.24) | copy-start | bytes 12292
  21.8 5.3 %copy-start.8 = (bf16[512,1024]{1,0:T(8,128)(2,1)S(1)}, bf16[512,1024]{1,0:T(8,128)(2,1)}, u32[]{:S(2)}) copy-start(bf16[512,1024]{1,0:T(8,128)(2,1)} %param.18) | copy-start | bytes 3145732
  26.5 24.6 %collective-permute-start.2 = (bf16[512,1024]{1,0:T(8,128)(2,1)S(1)}, bf16[512,1024]{1,0:T(8,128)(2,1)S(1)}, u32[]{:S(2)}, u32[]{:S(2)}) collective-permute-start(bf16[512,1024]{1,0:T(8,128)(2,1)S(1)} %collective-permute-done), channel_id=1, source_target_pairs={{0,1},{1,2},{2,3},{3,0},{4,5},{5,6},{6,7},{7,4},{8,9},{9,10},{10,1... | collective-permute-start | bytes 3145736 | tf_op jit(solution)/shard_map/ppermute | solution.py:22
  26.6 0.7 copy-start.20
  27.4 25.7 %copy-start.10 = (bf16[4096,16]{0,1:T(8,128)(2,1)S(1)}, bf16[4096,16]{0,1:T(8,128)(2,1)}, u32[]{:S(2)}) copy-start(bf16[4096,16]{0,1:T(8,128)(2,1)} %param.21) | copy-start | bytes 393220
  51.2 2.0 %copy-start.1 = (bf16[512,4096]{1,0:T(8,128)(2,1)}, bf16[512,4096]{1,0:T(8,128)(2,1)S(1)}, u32[]{:S(2)}) copy-start(bf16[512,4096]{1,0:T(8,128)(2,1)S(1)} %constant_dynamic-update-slice_fusion.2) | copy-start | bytes 12582916
  53.2 1.2 copy-start.16
  56.4 21.2 %collective-permute-start.4 = (f32[16]{0:T(128)S(1)}, f32[16]{0:T(128)S(1)}, u32[]{:S(2)}, u32[]{:S(2)}) collective-permute-start(f32[16]{0:T(128)S(1)} %reshape.274), channel_id=1, source_target_pairs={{0,4},{4,0},{8,12},{12,8},{16,20},{20,16},{24,28},{28,24},{32,36},... | collective-permute-start | bytes 200 | tf_op jit(solution)/shard_map/ppermute | solution.py:151
  58.7 15.9 %copy-start.2 = (bf16[512,4096]{1,0:T(8,128)(2,1)S(1)}, bf16[512,4096]{1,0:T(8,128)(2,1)}, u32[]{:S(2)}) copy-start(bf16[512,4096]{1,0:T(8,128)(2,1)} %copy-done.1) | copy-start | bytes 12582916
  58.7 15.9 %copy-start.18 = (bf16[4096,2,128]{2,1,0:T(2,128)(2,1)S(1)}, bf16[4096,2,128]{2,1,0:T(2,128)(2,1)}, u32[]{:S(2)}) copy-start(bf16[4096,2,128]{2,1,0:T(2,128)(2,1)} %param.20) | copy-start | bytes 6291460
  74.5 1.4 copy-start.4
  75.9 5.0 %copy-start.19 = (bf16[2,3,1024]{2,0,1:T(2,128)(2,1)S(1)}, bf16[2,3,1024]{2,0,1:T(2,128)(2,1)}, u32[]{:S(2)}) copy-start(bf16[2,3,1024]{2,0,1:T(2,128)(2,1)} %param.31) | copy-start | bytes 36868
  76.0 4.8 %collective-permute-start.3 = (bf16[2,3,1280]{2,0,1:T(2,128)(2,1)S(1)}, bf16[2,3,1280]{2,0,1:T(2,128)(2,1)S(1)}, u32[]{:S(2)}, u32[]{:S(2)}) collective-permute-start(bf16[2,3,1280]{2,0,1:T(2,128)(2,1)S(1)} %copy.107), channel_id=1, source_target_pairs={{0,4},{4,8},{8,12},{12,16},{16,20},{20,24},{24,28},{28,32},{32,36}... | collective-permute-start | bytes 46088 | tf_op jit(solution)/shard_map/ppermute | solution.py:35
  77.8 19.4 %collective-permute-start.5 = (f32[8]{0:T(128)S(1)}, f32[8]{0:T(128)S(1)}, u32[]{:S(2)}, u32[]{:S(2)}) collective-permute-start(f32[8]{0:T(128)S(1)} %reshape_squeeze.12), channel_id=1, source_target_pairs={{0,8},{4,12},{8,16},{12,20},{16,24},{20,28},{24,32},{28,36},{32,40... | collective-permute-start | bytes 104 | tf_op jit(solution)/shard_map/ppermute | solution.py:35
  79.5 17.7 %collective-permute-start.14 = (f32[8]{0:T(128)S(1)}, f32[8]{0:T(128)S(1)}, u32[]{:S(2)}, u32[]{:S(2)}) collective-permute-start(f32[8]{0:T(128)S(1)} %reshape_squeeze.14), channel_id=1, source_target_pairs={{0,8},{4,12},{8,16},{12,20},{16,24},{20,28},{24,32},{28,36},{32,40... | collective-permute-start | bytes 104 | tf_op jit(solution)/shard_map/ppermute | solution.py:35
  83.1 1.1 copy-start.3
  94.2 9.2 %collective-permute-start.8 = (f32[16,64,128]{2,1,0:T(8,128)S(1)}, f32[16,64,128]{2,1,0:T(8,128)S(1)}, u32[]{:S(2)}, u32[]{:S(2)}) collective-permute-start(f32[16,64,128]{2,1,0:T(8,128)S(1)} %bitcast.155), channel_id=1, source_target_pairs={{0,4},{4,0},{8,12},{12,8},{16,20},{20,16},{24,28},{28,24},{32,36},... | collective-permute-start | bytes 1572872 | tf_op jit(solution)/shard_map/ppermute | solution.py:151
  97.2 6.0 %collective-permute-start.6 = (f32[8]{0:T(128)S(1)}, f32[8]{0:T(128)S(1)}, u32[]{:S(2)}, u32[]{:S(2)}) collective-permute-start(f32[8]{0:T(128)S(1)} %get-tuple-element.18), channel_id=1, source_target_pairs={{0,16},{4,20},{8,24},{12,28},{16,32},{20,36},{24,40},{28,44},{32,4... | collective-permute-start | bytes 104 | tf_op jit(solution)/shard_map/ppermute | solution.py:35
  97.4 6.4 %collective-permute-start.15 = (f32[8]{0:T(128)S(1)}, f32[8]{0:T(128)S(1)}, u32[]{:S(2)}, u32[]{:S(2)}) collective-permute-start(f32[8]{0:T(128)S(1)} %get-tuple-element.25), channel_id=1, source_target_pairs={{0,16},{4,20},{8,24},{12,28},{16,32},{20,36},{24,40},{28,44},{32,4... | collective-permute-start | bytes 104 | tf_op jit(solution)/shard_map/ppermute | solution.py:35
  103.4 3.6 %collective-permute-start.7 = (f32[8]{0:T(128)S(1)}, f32[8]{0:T(128)S(1)}, u32[]{:S(2)}, u32[]{:S(2)}) collective-permute-start(f32[8]{0:T(128)S(1)} %fusion.58), channel_id=1, source_target_pairs={{0,32},{4,36},{8,40},{12,44},{16,48},{20,52},{24,56},{28,60},{32,6... | collective-permute-start | bytes 104 | tf_op jit(solution)/shard_map/ppermute | solution.py:35
  103.6 10.1 %collective-permute-start.9 = (f32[8,64,128]{2,1,0:T(8,128)S(1)}, f32[8,64,128]{2,1,0:T(8,128)S(1)}, u32[]{:S(2)}, u32[]{:S(2)}) collective-permute-start(f32[8,64,128]{2,1,0:T(8,128)S(1)} %bitcast.154), channel_id=1, source_target_pairs={{0,8},{4,12},{8,16},{12,20},{16,24},{20,28},{24,32},{28,36},{32,40... | collective-permute-start | bytes 786440 | tf_op jit(solution)/shard_map/ppermute | solution.py:35
  103.8 10.1 %collective-permute-start.16 = (f32[8]{0:T(128)S(1)}, f32[8]{0:T(128)S(1)}, u32[]{:S(2)}, u32[]{:S(2)}) collective-permute-start(f32[8]{0:T(128)S(1)} %fusion.60), channel_id=1, source_target_pairs={{0,32},{4,36},{8,40},{12,44},{16,48},{20,52},{24,56},{28,60},{32,6... | collective-permute-start | bytes 104 | tf_op jit(solution)/shard_map/ppermute | solution.py:35
  107.1 17.0 %collective-permute-start.13 = (f32[8]{0:T(128)S(1)}, f32[8]{0:T(128)S(1)}, u32[]{:S(2)}, u32[]{:S(2)}) collective-permute-start(f32[8]{0:T(128)S(1)} %fusion.53), channel_id=1, source_target_pairs={{0,64},{4,68},{8,72},{12,76},{16,80},{20,84},{24,88},{28,92},{32,9... | collective-permute-start | bytes 104 | tf_op jit(solution)/shard_map/ppermute | solution.py:35
  107.7 11.7 %collective-permute-start.17 = (f32[8,64,128]{2,1,0:T(8,128)S(1)}, f32[8,64,128]{2,1,0:T(8,128)S(1)}, u32[]{:S(2)}, u32[]{:S(2)}) collective-permute-start(f32[8,64,128]{2,1,0:T(8,128)S(1)} %bitcast.153), channel_id=1, source_target_pairs={{0,8},{4,12},{8,16},{12,20},{16,24},{20,28},{24,32},{28,36},{32,40... | collective-permute-start | bytes 786440 | tf_op jit(solution)/shard_map/ppermute | solution.py:35
  113.8 10.1 %collective-permute-start.10 = (f32[8,64,128]{2,1,0:T(8,128)S(1)}, f32[8,64,128]{2,1,0:T(8,128)S(1)}, u32[]{:S(2)}, u32[]{:S(2)}) collective-permute-start(f32[8,64,128]{2,1,0:T(8,128)S(1)} %multiply_add_fusion.5), channel_id=1, source_target_pairs={{0,16},{4,20},{8,24},{12,28},{16,32},{20,36},{24,40},{28,44},{32,4... | collective-permute-start | bytes 786440 | tf_op jit(solution)/shard_map/ppermute | solution.py:35
  114.0 18.1 %collective-permute-start.21 = (f32[8]{0:T(128)S(1)}, f32[8]{0:T(128)S(1)}, u32[]{:S(2)}, u32[]{:S(2)}) collective-permute-start(f32[8]{0:T(128)S(1)} %fusion.55), channel_id=1, source_target_pairs={{0,64},{4,68},{8,72},{12,76},{16,80},{20,84},{24,88},{28,92},{32,9... | collective-permute-start | bytes 104 | tf_op jit(solution)/shard_map/ppermute | solution.py:35
  119.5 10.1 %collective-permute-start.18 = (f32[8,64,128]{2,1,0:T(8,128)S(1)}, f32[8,64,128]{2,1,0:T(8,128)S(1)}, u32[]{:S(2)}, u32[]{:S(2)}) collective-permute-start(f32[8,64,128]{2,1,0:T(8,128)S(1)} %multiply_add_fusion.2), channel_id=1, source_target_pairs={{0,16},{4,20},{8,24},{12,28},{16,32},{20,36},{24,40},{28,44},{32,4... | collective-permute-start | bytes 786440 | tf_op jit(solution)/shard_map/ppermute | solution.py:35
  124.0 6.5 %collective-permute-start.11 = (f32[8,64,128]{2,1,0:T(8,128)S(1)}, f32[8,64,128]{2,1,0:T(8,128)S(1)}, u32[]{:S(2)}, u32[]{:S(2)}) collective-permute-start(f32[8,64,128]{2,1,0:T(8,128)S(1)} %multiply_add_fusion.4), channel_id=1, source_target_pairs={{0,32},{4,36},{8,40},{12,44},{16,48},{20,52},{24,56},{28,60},{32,6... | collective-permute-start | bytes 786440 | tf_op jit(solution)/shard_map/ppermute | solution.py:35
  129.7 9.0 %collective-permute-start.19 = (f32[8,64,128]{2,1,0:T(8,128)S(1)}, f32[8,64,128]{2,1,0:T(8,128)S(1)}, u32[]{:S(2)}, u32[]{:S(2)}) collective-permute-start(f32[8,64,128]{2,1,0:T(8,128)S(1)} %multiply_add_fusion.1), channel_id=1, source_target_pairs={{0,32},{4,36},{8,40},{12,44},{16,48},{20,52},{24,56},{28,60},{32,6... | collective-permute-start | bytes 786440 | tf_op jit(solution)/shard_map/ppermute | solution.py:35
  130.6 11.8 %collective-permute-start.12 = (f32[8,64,128]{2,1,0:T(8,128)S(1)}, f32[8,64,128]{2,1,0:T(8,128)S(1)}, u32[]{:S(2)}, u32[]{:S(2)}) collective-permute-start(f32[8,64,128]{2,1,0:T(8,128)S(1)} %multiply_add_fusion.3), channel_id=1, source_target_pairs={{0,64},{4,68},{8,72},{12,76},{16,80},{20,84},{24,88},{28,92},{32,9... | collective-permute-start | bytes 786440 | tf_op jit(solution)/shard_map/ppermute | solution.py:35
  138.8 10.1 %collective-permute-start.20 = (f32[8,64,128]{2,1,0:T(8,128)S(1)}, f32[8,64,128]{2,1,0:T(8,128)S(1)}, u32[]{:S(2)}, u32[]{:S(2)}) collective-permute-start(f32[8,64,128]{2,1,0:T(8,128)S(1)} %multiply_add_fusion), channel_id=1, source_target_pairs={{0,64},{4,68},{8,72},{12,76},{16,80},{20,84},{24,88},{28,92},{32,9... | collective-permute-start | bytes 786440 | tf_op jit(solution)/shard_map/ppermute | solution.py:35
  150.5 14.8 %collective-permute-start.22 = (f32[16,64,128]{2,1,0:T(8,128)}, f32[16,64,128]{2,1,0:T(8,128)}, u32[]{:S(2)}, u32[]{:S(2)}) collective-permute-start(f32[16,64,128]{2,1,0:T(8,128)} %get-tuple-element.31), channel_id=1, source_target_pairs={{0,4},{4,0},{8,12},{12,8},{16,20},{20,16},{24,28},{28,24},{32,36},... | collective-permute-start | bytes 1572872 | tf_op jit(solution)/shard_map/ppermute | solution.py:193
  162.6 4.2 %copy-start.9 = (f32[2,16,64,128]{3,0,2,1:T(2,128)S(1)}, f32[2,16,64,128]{3,0,2,1:T(2,128)}, u32[]{:S(2)}) copy-start(f32[2,16,64,128]{3,0,2,1:T(2,128)} %get-tuple-element.52) | copy-start | bytes 3145732
  166.8 2.9 %copy-start.6 = (bf16[2,256,1024]{1,2,0:T(8,128)(2,1)S(1)}, bf16[2,256,1024]{1,2,0:T(8,128)(2,1)}, u32[]{:S(2)}) copy-start(bf16[2,256,1024]{1,2,0:T(8,128)(2,1)} %copy.84) | copy-start | bytes 3145732
  166.8 2.9 %copy-start.7 = (f32[2,256,1024]{1,2,0:T(8,128)S(1)}, f32[2,256,1024]{1,2,0:T(8,128)}, u32[]{:S(2)}) copy-start(f32[2,256,1024]{1,2,0:T(8,128)} %copy.98) | copy-start | bytes 6291460
  166.8 2.9 %copy-start.21 = (f32[16]{0:T(128)S(1)}, f32[16]{0:T(128)}, u32[]{:S(2)}) copy-start(f32[16]{0:T(128)} %param.28) | copy-start | bytes 196
  179.6 2.1 %copy-start.5 = (bf16[512,2048]{1,0:T(8,128)(2,1)S(1)}, bf16[512,2048]{1,0:T(8,128)(2,1)}, u32[]{:S(2)}) copy-start(bf16[512,2048]{1,0:T(8,128)(2,1)} %copy-done.4) | copy-start | bytes 6291460
  179.6 2.1 %copy-start.12 = (f32[1024]{0:T(1024)S(1)}, f32[1024]{0:T(1024)}, u32[]{:S(2)}) copy-start(f32[1024]{0:T(1024)} %param.29) | copy-start | bytes 12292
